TPU v7x, 256 devices: a whole 4x4x8 slice. The times are simulated.
256 devices in a mesh: gx: 8 (over z), gy: 32 (over y, x, core).
Axes of the slice: x: 4, y: 4, z: 8, core: 2. Of those that a mesh axis runs over, the one named last changes fastest.
Arguments:
- lengths: int32 [17], replicated, may hold values from 16 to 16384, as said below
- page_table: int32 [1169], replicated, may hold values from 0 to 1287, as said below
- projected: bfloat16 [18432, 9216], P('gx', 'gy'), may hold values from -8 to 8
- residual: bfloat16 [18432, 3072], P('gx', 'gy'), may hold values from -6 to 6
- out_weight: bfloat16 [3072, 3072], P('gx', 'gy'), may hold values from -0.109375 to 0.109375
Outputs:
- hidden: bfloat16 [18432, 3072], P('gx', 'gy')
- cache_pages: bfloat16 [1288, 32, 3072], P('gx', 'gy')
Inputs may be any that keep to these rules, and one draw needn't show every extreme that they name: `lengths`: one prompt of 16384 tokens at a place drawn from the seed and 16 short prompts of 16 to 240 tokens; they sum to 18432. `page_table`: entry g is the physical page of logical page g (the pages of each prompt in order, 16 tokens each, prompts in packing order). Distinct logical pages in use get distinct physical pages, and such a page lies in [d * 161, (d + 1) * 161) where d is the index of gx whose tokens hold the page's first token. Entries past the last logical page in use are arbitrary; the last two entries are never in use and hold 0 and 1287.
All inputs are finite; a program needn't handle non-finite values.
Results may differ from a plain program's by a relative error of at most 0.012.
The roundings to bfloat16 on the way count: a program that leaves them out, or rounds other values in their place, can miss the bound.
Values may be sent and summed in bfloat16 or wider, within the bound.
No kernel may reach another device: no remote copies, remote signals or barrier semaphores. Data moves between devices by JAX's collectives and lax.ppermute only.
A program may use at most 128 MiB of HBM per device.

v0:
```python
from functools import partial
import math
import jax
import jax.numpy as jnp
from jax import lax
from jax.sharding import PartitionSpec as P

HD = 96
PAGE = 16


def passed_along(block, axis, distance):
    devices = range(lax.axis_size(axis))
    route = [(i - distance, i) for i in devices if i - distance in devices]
    return lax.ppermute(block, axis, route)


def segment_of(ends_at, token_index):
    return jnp.sum((ends_at[None, :] <= token_index[:, None]).astype(jnp.int32), axis=1)


def rotate(values, position):
    half_size = HD // 2
    inverse = 10000.0 ** (-(jnp.arange(half_size, dtype=jnp.float32) * 2.0) / HD)
    angle = position.astype(jnp.float32)[:, None, None] * inverse[None, None, :]
    cosine = jnp.cos(angle)
    sine_part = jnp.sin(angle)
    widened = values.astype(jnp.float32)
    front_half = widened[..., :half_size]
    back_half = widened[..., half_size:]
    turned = jnp.concatenate(
        [front_half * cosine - back_half * sine_part, back_half * cosine + front_half * sine_part],
        axis=-1,
    )
    return turned.astype(jnp.bfloat16)


def tile_update(
    query_block,
    query_segment,
    query_index,
    key_block,
    value_block,
    key_segment,
    key_index,
    carry_state,
):
    running_max, running_sum, running_acc = carry_state
    scores = jnp.einsum(
        "qhd,khd->hqk", query_block, key_block, preferred_element_type=jnp.float32
    ) * (1.0 / math.sqrt(HD))
    visible = (query_segment[:, None] == key_segment[None, :]) & (
        query_index[:, None] >= key_index[None, :]
    )
    scores = jnp.where(visible[None], scores, -1e30)
    new_max = jnp.maximum(running_max, jnp.max(scores, axis=2))
    weights = jnp.where(visible[None], jnp.exp(scores - new_max[:, :, None]), 0.0)
    factor = jnp.exp(running_max - new_max)
    new_sum = running_sum * factor + jnp.sum(weights, axis=2)
    new_acc = running_acc * factor[:, :, None] + jnp.einsum(
        "hqk,khd->hqd",
        weights.astype(jnp.bfloat16),
        value_block,
        preferred_element_type=jnp.float32,
    )
    return (new_max, new_sum, new_acc)


def keep_state(carry_state):
    return carry_state


def per_device(lengths, page_table, projected, residual, out_weight):
    row_count = projected.shape[0]
    local_heads = projected.shape[1] // (3 * HD)
    group_size = lax.axis_size("gx")
    group_index = lax.axis_index("gx")
    first_row = group_index * row_count
    ends_at = jnp.cumsum(lengths)
    starts_at = ends_at - lengths
    own_index = first_row + jnp.arange(row_count, dtype=jnp.int32)
    own_segment = segment_of(ends_at, own_index)
    own_position = own_index - starts_at[own_segment]
    split_heads = projected.reshape(row_count, local_heads, 3, HD)
    rotated_queries = rotate(split_heads[:, :, 0], own_position)
    rotated_keys = rotate(split_heads[:, :, 1], own_position)
    key_value = jnp.concatenate([rotated_keys, split_heads[:, :, 2]], axis=-1)
    half_rows = row_count // 2
    query_segment = segment_of(ends_at, own_index)
    query_rows = half_rows // max(1, half_rows // 576)
    block_count = row_count // query_rows
    query_blocks = [
        rotated_queries[number * query_rows : (number + 1) * query_rows]
        for number in range(block_count)
    ]
    initial = tuple(
        (
            (
                jnp.full((local_heads, query_rows), -1e30, jnp.float32),
                jnp.zeros((local_heads, query_rows), jnp.float32),
                jnp.zeros((local_heads, query_rows, HD), jnp.float32),
            )
            for number in range(block_count)
        )
    )
    portion = lax.all_gather(key_value, "gx", axis=0, tiled=True)
    key_count = portion.shape[0]
    key_rows = key_count // max(1, key_count // 1152)
    steps_needed = key_count // key_rows
    key_index = jnp.arange(key_count, dtype=jnp.int32)
    key_segment = segment_of(ends_at, key_index)
    scanned_input = (
        portion.reshape(steps_needed, key_rows, local_heads, 2 * HD),
        key_index.reshape(steps_needed, key_rows),
        key_segment.reshape(steps_needed, key_rows),
    )

    def advance(block_states, scanned):
        key_block, block_index, block_segment = scanned
        updated = []
        for number in range(block_count):
            lower_row = number * query_rows
            upper_row = lower_row + query_rows
            live = (block_index[0] <= own_index[upper_row - 1]) & (
                block_segment[key_rows - 1] >= query_segment[lower_row]
            )
            working = partial(
                tile_update,
                query_blocks[number],
                query_segment[lower_row:upper_row],
                own_index[lower_row:upper_row],
                key_block[:, :, :HD],
                key_block[:, :, HD:],
                block_segment,
                block_index,
            )
            updated.append(lax.cond(live, working, keep_state, block_states[number]))
        return (tuple(updated), None)

    folded = lax.scan(advance, initial, scanned_input)[0]
    pieces = []
    for number in range(block_count):
        running_max, running_sum, running_acc = folded[number]
        normalized = (running_acc / running_sum[:, :, None]).astype(jnp.bfloat16)
        pieces.append(jnp.swapaxes(normalized, 0, 1).reshape(query_rows, local_heads * HD))
    attended = jnp.concatenate(pieces, axis=0)
    weight_columns = lax.all_gather(out_weight, "gx", axis=0, tiled=True)
    update = jnp.dot(
        lax.all_gather(attended, "gy", axis=1, tiled=True),
        weight_columns,
        preferred_element_type=jnp.float32,
    )
    hidden = (residual.astype(jnp.float32) + update).astype(jnp.bfloat16)
    tail_rows = passed_along(key_value[: PAGE - 1], "gx", -1)
    extended = jnp.concatenate([key_value, tail_rows], axis=0)
    extended_index = first_row + jnp.arange(row_count + PAGE - 1, dtype=jnp.int32)
    extended_segment = jnp.minimum(segment_of(ends_at, extended_index), lengths.shape[0] - 1)
    extended_position = extended_index - starts_at[extended_segment]
    page_count = (lengths + PAGE - 1) // PAGE
    page_base = jnp.cumsum(page_count) - page_count
    logical = page_base[extended_segment] + extended_position // PAGE
    page_first = extended_index - extended_position % PAGE
    pages_held = row_count // PAGE + lengths.shape[0]
    owned = (page_first // row_count == group_index) & (extended_index < group_size * row_count)
    target = jnp.where(owned, page_table[logical] - group_index * pages_held, pages_held)
    cache_pages = jnp.zeros((pages_held, local_heads, PAGE, 2 * HD), jnp.bfloat16)
    cache_pages = cache_pages.at[target, :, extended_position % PAGE].set(extended, mode="drop")
    return (hidden, cache_pages.reshape(pages_held, local_heads, PAGE * 2 * HD))


def solution(mesh):
    placed = (P(), P(), P("gx", "gy"), P("gx", "gy"), P("gx", "gy"))
    return jax.shard_map(
        per_device,
        mesh=mesh,
        in_specs=placed,
        out_specs=(P("gx", "gy"), P("gx", "gy", None)),
        check_vma=False,
    )
```

profile of v0, /device:TPU:10, one launch (start us, length us, event | category | flops | bytes accessed | tf_op | source)
XLA Modules:
  0.0 589.0 jit_solution(8751553567018417610)
XLA Ops:
  7.2 0.7 copy.20
  8.8 0.7 fusion.105
  9.7 4.4 fusion.96
  14.4 1.4 fusion.83
  15.8 6.2 %fusion.92 = f32[2304]{0:T(1024)S(1)} fusion(pred[2304]{0:T(1024)(128)(4,1)S(1)} %get-tuple-element.388, pred[2304]{0:T(1024)(128)(4,1)S(1)} %get-tuple-element.387, pred[2304]{0:T(1024)(128)(4,1)S(1)} %get-tuple-element.386, pred[2304]{0:T(1024)(128)(4,1)S(1)} %get-tuple-element.385, pred[2304]{0:T(1024)(128)(4,1)S(1)} %get-tuple-element.384, ...), kind=kLoop, calls=%fused_computation.184 | loop fusion | flops 29952 | bytes 41516 | tf_op jit(solution)/shard_map/convert_element_type | solution.py:25
  22.0 2.0 fusion.82
  24.0 1.0 pad_maximum_fusion
  25.7 84.1 %all-gather.3.cloned.1.call-done = bf16[18432,1,192]{0,2,1:T(8,128)(2,1)} async-done(((bf16[2304,1,192]{0,2,1:T(8,128)(2,1)}), bf16[18432,1,192]{0,2,1:T(8,128)(2,1)}) %all-gather.3.cloned.1.call-update) | async-done | bytes 7077904 | tf_op jit(solution)/shard_map/all_gather | solution.py:106
  109.8 7.0 %copy.26 = bf16[1,24,16,8,1152]{4,3,1,0,2:T(8,128)(2,1)} copy(bf16[1,24,16,8,1152]{4,3,2,1,0:T(8,128)(2,1)} %bitcast.168) | data formatting | bytes 14155776 | tf_op jit(solution)/shard_map/reshape | solution.py:113
  117.0 229.6 %while.32 = (s32[]{:T(128)}, f32[1,576]{1,0:T(1,128)S(1)}, f32[1,576]{1,0:T(1,128)S(1)}, f32[1,576,96]{1,2,0:T(8,128)S(1)}, f32[1,576]{1,0:T(1,128)S(1)}, /*inde...) while((s32[]{:T(128)}, f32[1,576]{1,0:T(1,128)S(1)}, ...), condition=%wide.region_20.21_spmd, body=%wide.region_3.20_spmd.sunk | while | flops 1067440896 | bytes 37980108 | solution.py:140
  117.3 1.1 dynamic-slice_bitcast_fusion.2
  122.6 3.1 conditional.11
  122.8 1.0 fusion.100
  123.8 1.0 fusion.56
  124.8 0.9 fusion.50
  128.2 3.0 conditional.10
  128.3 1.0 fusion.99
  129.3 1.0 fusion.40
  130.3 0.9 fusion.34
  133.8 3.1 conditional.9
  134.0 1.0 fusion.98
  135.0 1.0 fusion.24
  136.0 0.9 fusion.18
  139.4 2.9 conditional.8
  139.5 1.0 fusion.97
  140.5 1.0 fusion.8
  141.4 0.9 fusion.2
  142.4 1.1 dynamic-slice_bitcast_fusion.2
  143.5 0.7 fusion.110
  147.8 3.1 conditional.11
  148.0 1.0 fusion.100
  149.0 1.0 fusion.56
  149.9 0.9 fusion.50
  153.4 2.9 conditional.10
  153.5 1.0 fusion.99
  154.5 1.0 fusion.40
  155.5 0.9 fusion.34
  161.6 1.1 dynamic-slice_bitcast_fusion.2
  174.9 1.1 dynamic-slice_bitcast_fusion.2
  188.1 1.1 dynamic-slice_bitcast_fusion.2
  201.3 1.1 dynamic-slice_bitcast_fusion.2
  214.5 1.1 dynamic-slice_bitcast_fusion.2
  227.7 1.1 dynamic-slice_bitcast_fusion.2
  240.9 1.1 dynamic-slice_bitcast_fusion.2
  254.2 1.1 dynamic-slice_bitcast_fusion.2
  267.4 1.1 dynamic-slice_bitcast_fusion.2
  280.6 1.1 dynamic-slice_bitcast_fusion.2
  293.8 1.1 dynamic-slice_bitcast_fusion.2
  307.0 1.1 dynamic-slice_bitcast_fusion.2
  320.2 1.1 dynamic-slice_bitcast_fusion.2
  333.4 1.1 dynamic-slice_bitcast_fusion.2
  346.8 1.0 concatenate.37
  347.8 0.8 slice.201
  348.6 1.5 collective-permute-start
  350.4 0.7 fusion.104
  351.2 8.8 %fusion.93 = (s32[2319]{0:T(1024)S(1)}, s32[2319]{0:T(1024)S(1)}, s32[2319,1]{0,1:T(1,128)S(1)}) fusion(s32[]{:T(128)} %bitcast.66, s32[]{:T(128)} %bitcast.67, s32[]{:T(128)} %bitcast.68, s32[]{:T(128)} %bitcast.69, s32[]{:T(128)} %bitcast.70, s32[]{:T(128)} %bitcast.72, s32[]{:T(128)} %bitcast.71, s32[]{:T(128)} %bitcast.46, s32[]{:T(128)} %bitcast.45, ...), kind=kLoop, calls=%fused_computation.187 | loop fusion | flops 48699 | bytes 37160 | tf_op jit(solution)/shard_map/gather | solution.py:161
  360.4 6.2 %select_select_fusion.1 = s32[2319]{0:T(1024)S(1)} fusion(pred[2319]{0:T(1024)(128)(4,1)S(1)} %get-tuple-element.378, pred[2319]{0:T(1024)(128)(4,1)S(1)} %get-tuple-element.377, pred[2319]{0:T(1024)(128)(4,1)S(1)} %get-tuple-element.376, pred[2319]{0:T(1024)(128)(4,1)S(1)} %get-tuple-element.375, pred[2319]{0:T(1024)(128)(4,1)S(1)} %get-tuple-element.374, ...), kind=kLoop, calls=%fused_computation.182 | loop fusion | flops 23190 | bytes 41782 | tf_op jit(solution)/shard_map/gather | solution.py:158
  366.6 6.5 %select_select_fusion = s32[2319]{0:T(1024)S(1)} fusion(pred[2319]{0:T(1024)(128)(4,1)S(1)} %get-tuple-element.378, pred[2319]{0:T(1024)(128)(4,1)S(1)} %get-tuple-element.377, pred[2319]{0:T(1024)(128)(4,1)S(1)} %get-tuple-element.376, pred[2319]{0:T(1024)(128)(4,1)S(1)} %get-tuple-element.375, pred[2319]{0:T(1024)(128)(4,1)S(1)} %get-tuple-element.374, ...), kind=kLoop, calls=%fused_computation.181 | loop fusion | flops 23190 | bytes 41782 | tf_op jit(solution)/shard_map/gather | solution.py:161
  373.3 12.7 %gather_fusion = s32[2319]{0:T(1024)S(1)} fusion(s32[1169]{0:T(1024)S(1)} %copy-done, s32[3072]{0:T(1024)S(1)} %pad_clamp_fusion), kind=kCustom, calls=%fused_computation | custom fusion | bytes 27828 | tf_op jit(solution)/shard_map/gather | solution.py:165
  386.4 169.8 %all_gather.11 = bf16[3072,96]{0,1:T(8,128)(2,1)S(1)} all-gather(bf16[384,96]{0,1:T(8,128)(2,1)S(1)} %copy-done.2), channel_id=1, replica_groups=mesh['gx'=8,'gy'=32] {'gx'}, dimensions={0}, use_global_device_ids=true | all-gather | bytes 663552 | tf_op jit(solution)/shard_map/all_gather | solution.py:147
  556.3 1.6 copy.23
  557.9 13.5 %scatter_custom_fusion = bf16[2576,192]{1,0:T(8,128)(2,1)S(1)} fusion(s32[2319]{0:T(1024)S(1)} %broadcast_select_fusion, bf16[2319,192]{1,0:T(8,128)(2,1)} %copy.23, bf16[]{:T(256)} %constant.123.clone.1), kind=kCustom, calls=%fused_computation.81 | custom fusion | bytes 989696
  571.4 2.5 reshape.620
  573.9 8.2 %fusion.64 = bf16[2304,96]{0,1:T(8,128)(2,1)} fusion(bf16[3072,96]{0,1:T(8,128)(2,1)S(1)} %all_gather.11, bf16[2304,3072]{0,1:T(8,128)(2,1)} %all-gather.5.cloned.1.call-done, bf16[2304,96]{0,1:T(8,128)(2,1)S(1)} %copy-done.1), kind=kOutput, calls=%fused_computation.76 | convolution fusion | flops 1359618048 | bytes 15630336 | tf_op jit(solution)/shard_map/dot_general | solution.py:148
  (228 shorter events, 35.3 us)
Async XLA Ops:
  7.2 366.1 %copy-start = (s32[1169]{0:T(1024)S(1)}, s32[1169]{0:T(1024)}, u32[]{:S(2)}) copy-start(s32[1169]{0:T(1024)} %param.16) | copy-start | bytes 14032
  7.2 102.7 %all-gather.3.cloned.1.call-start = ((), (), s32[]{:S(2)}) async-start(), calls=%async_computation | async-start | bytes 7962624 | tf_op jit(solution)/shard_map/all_gather | solution.py:106
  25.0 548.9 %all-gather.5.cloned.1.call-start = ((), (), s32[]{:S(2)}) async-start(), calls=%async_computation.1 | async-start | bytes 14598144 | tf_op jit(solution)/shard_map/all_gather | solution.py:149
  348.6 207.6 %collective-permute-start = (bf16[15,1,192]{0,2,1:T(8,128)(2,1)S(1)}, bf16[15,1,192]{0,2,1:T(8,128)(2,1)S(1)}, u32[]{:S(2)}, u32[]{:S(2)}) collective-permute-start(bf16[15,1,192]{0,2,1:T(8,128)(2,1)S(1)} %slice.201), channel_id=1, source_target_pairs={{32,0},{64,32},{96,64},{128,96},{160,128},{192,160},{224,192},{33,... | collective-permute-start | bytes 17288 | tf_op jit(solution)/shard_map/ppermute | solution.py:15
  373.2 12.9 %copy-start.3 = (s32[2]{0:T(128)S(1)}, s32[2]{0:T(128)}, u32[]{:S(2)}) copy-start(s32[2]{0:T(128)} %constant.132) | copy-start | bytes 28
  373.3 13.0 %copy-start.4 = (s32[2]{0:T(128)S(1)}, s32[2]{0:T(128)}, u32[]{:S(2)}) copy-start(s32[2]{0:T(128)} %constant.135) | copy-start | bytes 28
  373.3 13.1 %copy-start.2 = (bf16[384,96]{0,1:T(8,128)(2,1)S(1)}, bf16[384,96]{0,1:T(8,128)(2,1)}, u32[]{:S(2)}) copy-start(bf16[384,96]{0,1:T(8,128)(2,1)} %param.19) | copy-start | bytes 221188
  556.3 17.7 %copy-start.1 = (bf16[2304,96]{0,1:T(8,128)(2,1)S(1)}, bf16[2304,96]{0,1:T(8,128)(2,1)}, u32[]{:S(2)}) copy-start(bf16[2304,96]{0,1:T(8,128)(2,1)} %param.18) | copy-start | bytes 1327108
Sparse Core Ops, SparseCore 0:
  25.2 84.6 all-gather.2
  347.9 211.4 all-gather.4
where the time goes:
time: 593 us; the launch traced here: 589 us
  blocking collectives  170 us (29%)
  loops' own time  164 us (28%)
  local copies, waits for them, and re-layouts  89.9 us (15%)
  waiting for transfers between devices  84.2 us (14%)
  other arithmetic  45.2 us (8%)
  matrix products  19.9 us (3%)
  between operations  14.4 us (2%)
    all_gather x1, blocking collectives, per_device(): weight_columns = lax.all_gather(out_weight, 'gx', axis=0, tiled=True)  170 us
    another operation x1, loops' own time, per_device(): folded = lax.scan(advance, initial, scanned_input)[0]  163 us
    all_gather x1, waiting for transfers between devices, per_device(): portion = lax.all_gather(key_value, 'gx', axis=0, tiled=True)  84.1 us
    squeeze x16, local copies, waits for them, and re-layouts, per_device(): folded = lax.scan(advance, initial, scanned_input)[0]  16.9 us
    gather x2, other arithmetic, per_device(): logical = page_base[extended_segment] + extended_position // PAGE  15.4 us
    unnamed x11, local copies, waits for them, and re-layouts  13.6 us
    gather x1, local copies, waits for them, and re-layouts, per_device(): page_table[logical] - group_index * pages_held  12.7 us
  transfers between devices with their start and end apart: 3, of which 1 were waited for; matrix products, arithmetic and copies ran while one was open for 9% of the time, Pallas kernels for 0%

commit v1 on v0

--- a/solution.py
+++ b/solution.py
@@ -103,7 +103,9 @@
             for number in range(block_count)
         )
     )
-    portion = lax.all_gather(key_value, "gx", axis=0, tiled=True)
+    portion = jnp.concatenate(
+        lax.all_to_all(jnp.stack([key_value] * lax.axis_size("gx")), "gx", 0, 0), axis=0
+    )
     key_count = portion.shape[0]
     key_rows = key_count // max(1, key_count // 1152)
     steps_needed = key_count // key_rows

time: 593 us -> 746 us (1.26)
  waiting for transfers between devices: 84.2 us -> 157 us
  blocking collectives: 170 us -> 211 us
  local copies, waits for them, and re-layouts: 89.9 us -> 114 us
  starting transfers between devices: 1.58 us -> 10 us
    all_to_all x0 -> x1, waiting for transfers between devices: none -> 157 us  [per_device(): lax.all_to_all(jnp.stack([key_value] * lax.axis_size('gx')), 'gx', 0, 0)]
    all_gather x1 -> x0, waiting for transfers between devices: 84.1 us -> none  [per_device(): portion = lax.all_gather(key_value, 'gx', axis=0, tiled=True)]
    all_gather x1, blocking collectives: 170 us -> 211 us  [per_device(): weight_columns = lax.all_gather(out_weight, 'gx', axis=0, tiled=True)]
    another operation x14 -> x16, local copies, waits for them, and re-layouts: 0.95 us -> 15.4 us  [the longest x1 11.1 us: per_device(): portion.reshape(steps_needed, key_rows, local_heads, 2 * HD)]
    all_to_all x0 -> x1, local copies, waits for them, and re-layouts: none -> 9.82 us  [per_device(): lax.all_to_all(jnp.stack([key_value] * lax.axis_size('gx')), 'gx', 0, 0)]
    all_to_all x0 -> x1, starting transfers between devices: none -> 8.47 us  [per_device(): lax.all_to_all(jnp.stack([key_value] * lax.axis_size('gx')), 'gx', 0, 0)]
    while x0 -> x1, local copies, waits for them, and re-layouts: none -> 7.59 us  [per_device(): folded = lax.scan(advance, initial, scanned_input)[0]]
  transfers between devices with their start and end apart: 3 -> 3, of which waited for: 1 -> 1; matrix products, arithmetic and copies ran while one was open for 9% -> 7% of each run, Pallas kernels for 0% -> 0%
where the time goes in v1:
time: 746 us; the launch traced here: 741 us
  blocking collectives  211 us (28%)
  loops' own time  164 us (22%)
  waiting for transfers between devices  157 us (21%)
  local copies, waits for them, and re-layouts  114 us (15%)
  other arithmetic  44.7 us (6%)
  matrix products  25.3 us (3%)
  between operations  14.4 us (2%)
  starting transfers between devices  10 us (1%)
    all_gather x1, blocking collectives, per_device(): weight_columns = lax.all_gather(out_weight, 'gx', axis=0, tiled=True)  211 us
    another operation x1, loops' own time, per_device(): folded = lax.scan(advance, initial, scanned_input)[0]  163 us
    all_to_all x1, waiting for transfers between devices, per_device(): lax.all_to_all(jnp.stack([key_value] * lax.axis_size('gx')), 'gx', 0, 0)  157 us
    squeeze x16, local copies, waits for them, and re-layouts, per_device(): folded = lax.scan(advance, initial, scanned_input)[0]  16.9 us
    gather x2, other arithmetic, per_device(): logical = page_base[extended_segment] + extended_position // PAGE  15 us
  transfers between devices with their start and end apart: 3, of which 1 were waited for; matrix products, arithmetic and copies ran while one was open for 7% of the time, Pallas kernels for 0%

profile of v1, /device:TPU:10, one launch (start us, length us, event | category | flops | bytes accessed | tf_op | source)
XLA Modules:
  0.0 740.7 jit_solution(9168482104039588510)
XLA Ops:
  7.2 0.7 copy.25
  9.6 4.4 fusion.96
  14.3 1.4 fusion.83
  15.7 6.2 fusion.92
  22.0 2.0 fusion.82
  24.1 3.4 stack.2
  27.5 8.5 %all-to-all-start = ((bf16[8,2304,1,192]{1,3,2,0:T(8,128)(2,1)}), bf16[8,2304,1,192]{1,3,2,0:T(8,128)(2,1)}, u32[]{:S(2)}, u32[]{:S(2)}) async-start(bf16[8,2304,1,192]{1,3,2,0:T(8,128)(2,1)} %stack.2), calls=%async_computation | async-start | bytes 14155776 | tf_op jit(solution)/shard_map/all_to_all | solution.py:107
  36.4 0.8 pad_maximum_fusion.1
  37.3 157.1 %all-to-all-done = bf16[8,2304,1,192]{1,3,2,0:T(8,128)(2,1)} async-done(((bf16[8,2304,1,192]{1,3,2,0:T(8,128)(2,1)}), bf16[8,2304,1,192]{1,3,2,0:T(8,128)(2,1)}, u32[]{:S(2)}, u32[]{:S(2)}) %all-to-all-start) | async-done | bytes 7077920 | tf_op jit(solution)/shard_map/all_to_all | solution.py:107
  194.4 9.8 %copy.26 = bf16[8,2304,1,192]{1,0,3,2:T(8,128)(2,1)} copy(bf16[8,2304,1,192]{1,3,2,0:T(8,128)(2,1)} %all-to-all-done) | data formatting | bytes 14155776 | tf_op jit(solution)/shard_map/all_to_all | solution.py:107
  204.2 11.1 %reshape_reshape.3 = bf16[16,1152,1,192]{1,0,3,2:T(8,128)(2,1)} reshape(bf16[8,2304,1,192]{1,0,3,2:T(8,128)(2,1)} %copy.26) | data formatting | bytes 14155776 | tf_op jit(solution)/shard_map/reshape;reshape | solution.py:115
  215.3 7.6 %copy.27 = bf16[16,1152,1,192]{1,3,2,0:T(8,128)(2,1)} copy(bf16[16,1152,1,192]{1,0,3,2:T(8,128)(2,1)} %reshape_reshape.3) | data formatting | bytes 14155776 | tf_op jit(solution)/shard_map/while | solution.py:142
  223.1 235.0 %while.32 = (s32[]{:T(128)}, f32[1,576]{1,0:T(1,128)S(1)}, f32[1,576]{1,0:T(1,128)S(1)}, f32[1,576,96]{1,2,0:T(8,128)S(1)}, f32[1,576]{1,0:T(1,128)S(1)}, /*inde...) while((s32[]{:T(128)}, f32[1,576]{1,0:T(1,128)S(1)}, ...), condition=%wide.region_20.21_spmd, body=%wide.region_3.20_spmd.sunk | while | flops 1067440896 | bytes 37980108 | solution.py:142
  223.3 1.1 dynamic-slice_bitcast_fusion.2
  228.7 4.0 conditional.11
  228.8 1.9 fusion.101
  230.7 1.0 fusion.56
  231.7 0.9 fusion.50
  235.2 3.9 conditional.10
  235.2 1.9 fusion.100
  237.2 1.0 fusion.40
  238.1 0.9 fusion.34
  241.7 4.0 conditional.9
  241.9 1.9 fusion.99
  243.8 1.0 fusion.24
  244.8 0.9 fusion.18
  248.2 3.9 conditional.8
  248.2 1.9 fusion.98
  250.1 1.0 fusion.8
  251.1 0.9 fusion.2
  252.1 1.1 dynamic-slice_bitcast_fusion.2
  257.5 4.0 conditional.11
  257.7 1.9 fusion.101
  259.6 1.0 fusion.56
  260.5 0.9 fusion.50
  264.0 3.9 conditional.10
  264.1 1.9 fusion.100
  266.0 1.0 fusion.40
  267.0 0.9 fusion.34
  273.2 1.1 dynamic-slice_bitcast_fusion.2
  286.4 1.1 dynamic-slice_bitcast_fusion.2
  299.6 1.1 dynamic-slice_bitcast_fusion.2
  312.8 1.1 dynamic-slice_bitcast_fusion.2
  326.0 1.1 dynamic-slice_bitcast_fusion.2
  339.2 1.1 dynamic-slice_bitcast_fusion.2
  352.4 1.1 dynamic-slice_bitcast_fusion.2
  365.7 1.1 dynamic-slice_bitcast_fusion.2
  378.9 1.1 dynamic-slice_bitcast_fusion.2
  392.1 1.1 dynamic-slice_bitcast_fusion.2
  405.3 1.1 dynamic-slice_bitcast_fusion.2
  418.5 1.1 dynamic-slice_bitcast_fusion.2
  431.7 1.1 dynamic-slice_bitcast_fusion.2
  445.0 1.1 dynamic-slice_bitcast_fusion.2
  458.3 1.0 concatenate.40
  459.3 1.5 collective-permute-start
  462.0 8.8 %fusion.93 = (s32[2319]{0:T(1024)S(1)}, s32[2319]{0:T(1024)S(1)}, s32[2319,1]{0,1:T(1,128)S(1)}) fusion(s32[]{:T(128)} %bitcast.67, s32[]{:T(128)} %bitcast.68, s32[]{:T(128)} %bitcast.69, s32[]{:T(128)} %bitcast.70, s32[]{:T(128)} %bitcast.71, s32[]{:T(128)} %bitcast.73, s32[]{:T(128)} %bitcast.72, s32[]{:T(128)} %bitcast.46, s32[]{:T(128)} %bitcast.45, ...), kind=kLoop, calls=%fused_computation.186 | loop fusion | flops 48699 | bytes 37160 | tf_op jit(solution)/shard_map/gather | solution.py:163
  471.0 6.2 select_select_fusion.1
  477.3 6.2 select_select_fusion
  483.7 12.7 %gather_fusion = s32[2319]{0:T(1024)S(1)} fusion(s32[1169]{0:T(1024)S(1)} %copy-done, s32[3072]{0:T(1024)S(1)} %pad_clamp_fusion), kind=kCustom, calls=%fused_computation | custom fusion | bytes 27828 | tf_op jit(solution)/shard_map/gather | solution.py:167
  496.8 211.1 %all_gather.7 = bf16[3072,96]{0,1:T(8,128)(2,1)S(1)} all-gather(bf16[384,96]{0,1:T(8,128)(2,1)S(1)} %copy-done.2), channel_id=1, replica_groups=mesh['gx'=8,'gy'=32] {'gx'}, dimensions={0}, use_global_device_ids=true | all-gather | bytes 663552 | tf_op jit(solution)/shard_map/all_gather | solution.py:149
  708.0 1.6 copy.29
  709.6 13.5 %scatter_custom_fusion = bf16[2576,192]{1,0:T(8,128)(2,1)S(1)} fusion(s32[2319]{0:T(1024)S(1)} %broadcast_select_fusion, bf16[2319,192]{1,0:T(8,128)(2,1)} %copy.29, bf16[]{:T(256)} %constant.123.clone.1), kind=kCustom, calls=%fused_computation.80 | custom fusion | bytes 989696
  723.1 2.5 reshape.619
  725.6 8.2 %fusion.64 = bf16[2304,96]{0,1:T(8,128)(2,1)} fusion(bf16[3072,96]{0,1:T(8,128)(2,1)S(1)} %all_gather.7, bf16[2304,3072]{0,1:T(8,128)(2,1)} %all-gather.2.cloned.1.call-done, bf16[2304,96]{0,1:T(8,128)(2,1)S(1)} %copy-done.1), kind=kOutput, calls=%fused_computation.75 | convolution fusion | flops 1359618048 | bytes 15630336 | tf_op jit(solution)/shard_map/dot_general | solution.py:150
  (230 shorter events, 37.3 us)
Async XLA Ops:
  7.2 476.5 %copy-start = (s32[1169]{0:T(1024)S(1)}, s32[1169]{0:T(1024)}, u32[]{:S(2)}) copy-start(s32[1169]{0:T(1024)} %param.16) | copy-start | bytes 14032
  27.5 166.9 %all-to-all-start = ((bf16[8,2304,1,192]{1,3,2,0:T(8,128)(2,1)}), bf16[8,2304,1,192]{1,3,2,0:T(8,128)(2,1)}, u32[]{:S(2)}, u32[]{:S(2)}) async-start(bf16[8,2304,1,192]{1,3,2,0:T(8,128)(2,1)} %stack.2), calls=%async_computation | async-start | bytes 14155776 | tf_op jit(solution)/shard_map/all_to_all | solution.py:107
  36.0 689.6 %all-gather.2.cloned.1.call-start = ((), (), s32[]{:S(2)}) async-start(), calls=%async_computation.1 | async-start | bytes 14598144 | tf_op jit(solution)/shard_map/all_gather | solution.py:151
  459.3 248.6 %collective-permute-start = (bf16[15,1,192]{0,2,1:T(8,128)(2,1)S(1)}, bf16[15,1,192]{0,2,1:T(8,128)(2,1)S(1)}, u32[]{:S(2)}, u32[]{:S(2)}) collective-permute-start(bf16[15,1,192]{0,2,1:T(8,128)(2,1)S(1)} %slice.201), channel_id=1, source_target_pairs={{32,0},{64,32},{96,64},{128,96},{160,128},{192,160},{224,192},{33,... | collective-permute-start | bytes 17288 | tf_op jit(solution)/shard_map/ppermute | solution.py:15
  483.6 12.9 %copy-start.3 = (s32[2]{0:T(128)S(1)}, s32[2]{0:T(128)}, u32[]{:S(2)}) copy-start(s32[2]{0:T(128)} %constant.132) | copy-start | bytes 28
  483.7 13.0 %copy-start.4 = (s32[2]{0:T(128)S(1)}, s32[2]{0:T(128)}, u32[]{:S(2)}) copy-start(s32[2]{0:T(128)} %constant.135) | copy-start | bytes 28
  483.7 13.1 %copy-start.2 = (bf16[384,96]{0,1:T(8,128)(2,1)S(1)}, bf16[384,96]{0,1:T(8,128)(2,1)}, u32[]{:S(2)}) copy-start(bf16[384,96]{0,1:T(8,128)(2,1)} %param.19) | copy-start | bytes 221188
  708.0 17.6 %copy-start.1 = (bf16[2304,96]{0,1:T(8,128)(2,1)S(1)}, bf16[2304,96]{0,1:T(8,128)(2,1)}, u32[]{:S(2)}) copy-start(bf16[2304,96]{0,1:T(8,128)(2,1)} %param.18) | copy-start | bytes 1327108
Sparse Core Ops, SparseCore 0:
  459.4 253.1 all-gather.1
